TPU v7x, 512 devices: a whole 4x4x16 slice. The times are simulated.
512 devices in a mesh: row: 32 (over x, z_hi, core), col: 16 (over z_lo, y).
Axes of the slice: x: 4, y: 4, z: 16 (z_hi: 4, z_lo: 4; z = z_hi * 4 + z_lo), core: 2. Of those that a mesh axis runs over, the one named last changes fastest.
Arguments:
- images: bfloat16 [32, 128, 128, 256], P('row', 'col'), may hold values from -6 to 6
- weight: bfloat16 [3, 3, 256, 256], P(None, None, None, 'col'), may hold values from -0.125 to 0.125
- norm_gain: float32 [256], replicated, may hold values from 0.5 to 1.5
- cotangent: bfloat16 [32, 128, 128, 256], P('row', 'col'), may hold values from -6 to 6
Outputs:
- features: bfloat16 [32, 128, 128, 256], P('row', 'col')
- input_grad: bfloat16 [32, 128, 128, 256], P('row', 'col')
- weight_grad: float32 [3, 3, 256, 256], P(None, None, None, 'col')
All inputs are finite; a program needn't handle non-finite values.
Results may differ from a plain program's by a relative error of at most 0.013.
Values may be sent and summed in bfloat16 or wider, within the bound.
No kernel may reach another device: no remote copies, remote signals or barrier semaphores. Data moves between devices by JAX's collectives and lax.ppermute only.
A program may use at most 64 MiB of HBM per device.

v0:
```python
import math
import jax
import jax.numpy as jnp
from jax import lax
from jax.sharding import PartitionSpec as P

epsilon = 1e-06
root_half = 0.7071067811865476
norm_const = 0.3989422804014327


def padded_2(value, sides, width):
    for axis, dim in sides:
        peers, length = (lax.axis_size(axis), value.shape[dim])
        up = [(i, (i + 1) % peers) for i in range(peers - 1)]
        down = [(j, i) for i, j in up]
        last = lax.slice_in_dim(value, length - width, length, axis=dim)
        initial = lax.slice_in_dim(value, 0, width, axis=dim)
        before = lax.ppermute(last, axis, up)
        after = lax.ppermute(initial, axis, down)
        value = jnp.concatenate([before, value, after], axis=dim)
    return value


def norm_act(conv_out, upper, norm_gain):
    mean_val = jnp.mean(conv_out, axis=-1, keepdims=True)
    centred = conv_out - mean_val
    variance = jnp.mean(centred * centred, axis=-1, keepdims=True)
    inv_std = lax.rsqrt(variance + epsilon)
    unit = centred * inv_std
    normed = unit * norm_gain
    cdf_val = 0.5 * (1.0 + lax.erf(normed * root_half))
    density = jnp.exp(-0.5 * normed * normed) * norm_const
    outputs = (normed * cdf_val).astype(jnp.bfloat16)
    upstream = upper.astype(jnp.float32) * (cdf_val + normed * density) * norm_gain
    mean_up = jnp.mean(upstream, axis=-1, keepdims=True)
    mean_cross = jnp.mean(upstream * unit, axis=-1, keepdims=True)
    grad_pre = inv_std * (upstream - mean_up - unit * mean_cross)
    return (outputs, grad_pre.astype(jnp.bfloat16))


def window(padded, tap_row, tap_col, tile_rows, tile_cols):
    return padded[:, tap_row : tap_row + tile_rows, tap_col : tap_col + tile_cols, :].reshape(
        -1, padded.shape[-1]
    )


def on_device(images, weight, norm_gain, cotangent):
    img_count, tile_rows, tile_cols, in_chan = images.shape
    whole_kernel = lax.all_gather(weight, "col", axis=3, tiled=True)
    out_chan = whole_kernel.shape[3]
    rimmed = padded_2(images, (("col", 1),), 1)
    padded = jnp.pad(rimmed, ((0, 0), (0, 0), (1, 1), (0, 0)))
    conv_out = jnp.zeros((img_count * tile_rows * tile_cols, out_chan), jnp.float32)
    for tap_row in range(3):
        for tap_col in range(3):
            conv_out = conv_out + jnp.dot(
                window(padded, tap_row, tap_col, tile_rows, tile_cols),
                whole_kernel[tap_row, tap_col],
                preferred_element_type=jnp.float32,
            )
    outputs, grad_pre = norm_act(conv_out, cotangent.reshape(-1, out_chan), norm_gain)
    grad_grid = grad_pre.reshape(img_count, tile_rows, tile_cols, out_chan)
    grad_rimmed = padded_2(grad_grid, (("col", 1),), 1)
    grad_pad = jnp.pad(grad_rimmed, ((0, 0), (0, 0), (1, 1), (0, 0)))
    grad_input = jnp.zeros((img_count * tile_rows * tile_cols, in_chan), jnp.float32)
    pieces = []
    for tap_row in range(3):
        for tap_col in range(3):
            grad_input = grad_input + lax.dot_general(
                window(grad_pad, 2 - tap_row, 2 - tap_col, tile_rows, tile_cols),
                whole_kernel[tap_row, tap_col],
                (((1,), (1,)), ((), ())),
                preferred_element_type=jnp.float32,
            )
            pieces.append(
                lax.dot_general(
                    window(padded, tap_row, tap_col, tile_rows, tile_cols),
                    grad_pre,
                    (((0,), (0,)), ((), ())),
                    preferred_element_type=jnp.float32,
                )
            )
    partial_value = jnp.stack(pieces).reshape(3, 3, in_chan, out_chan)
    totals = lax.psum(partial_value, ("row", "col"))
    col_share = out_chan // lax.axis_size("col")
    own_share = lax.dynamic_slice_in_dim(totals, lax.axis_index("col") * col_share, col_share, 3)
    pixels = img_count * lax.axis_size("row") * tile_rows * lax.axis_size("col") * tile_cols
    weight_grad = own_share * (1.0 / math.sqrt(pixels))
    features = outputs.reshape(img_count, tile_rows, tile_cols, out_chan)
    input_grad = grad_input.astype(jnp.bfloat16).reshape(img_count, tile_rows, tile_cols, in_chan)
    return (features, input_grad, weight_grad)


def solution(mesh):
    placed = (
        P("row", "col", None, None),
        P(None, None, None, "col"),
        P(),
        P("row", "col", None, None),
    )
    return jax.shard_map(
        on_device,
        mesh=mesh,
        in_specs=placed,
        out_specs=(
            P("row", "col", None, None),
            P("row", "col", None, None),
            P(None, None, None, "col"),
        ),
        check_vma=False,
    )
```

profile of v0, /device:TPU:2, one launch (start us, length us, event | category | flops | bytes accessed | tf_op | source)
XLA Modules:
  0.0 616.7 jit_solution(12036107945683514388)
XLA Ops:
  7.2 0.7 all-gather.2.cloned.1.call-update
  8.0 0.9 fusion.29
  8.8 3.5 collective-permute-start
  12.3 1.3 collective-permute-start.1
  13.6 0.6 collective-permute-done
  14.2 4.3 collective-permute-done.1
  18.5 1.2 select_maximum_fusion.2
  19.7 1.0 pad_maximum_fusion.2
  20.8 1.4 fusion.27
  22.1 79.2 %all-gather.2.cloned.1.call-done = bf16[3,3,256,256]{2,3,1,0:T(8,128)(2,1)} async-done(((bf16[3,3,256,16]{2,3,1,0:T(8,128)(2,1)}), bf16[3,3,256,256]{2,3,1,0:T(8,128)(2,1)}) %all-gather.2.cloned.1.call-update) | async-done | bytes 1179664 | tf_op jit(solution)/shard_map/all_gather | solution.py:50
  101.3 1.4 fusion.21
  102.7 0.3 fusion.23
  103.0 0.3 convolution_add_fusion.13
  103.4 0.7 copy-done.6
  104.0 0.3 convolution_add_fusion.12
  104.4 0.3 convolution_add_fusion.11
  104.8 0.3 convolution_add_fusion.10
  105.1 0.7 copy-done.4
  105.8 0.3 convolution_add_fusion.9
  106.2 0.3 convolution_add_fusion.8
  106.5 0.7 copy-done.7
  107.2 0.4 fusion.30
  107.7 0.4 multiply_reduce_fusion.1
  108.1 0.6 copy-done.9
  108.7 1.9 fusion.24
  110.6 0.8 multiply_convert_fusion
  111.5 1.0 fusion.12
  112.5 1.1 fusion.11
  113.5 1.1 fusion.10
  114.6 1.1 fusion.9
  115.7 1.0 fusion.8
  116.7 1.0 fusion.7
  117.8 1.0 fusion.6
  118.8 1.0 fusion.5
  119.8 3.0 collective-permute-start.2
  122.9 1.3 collective-permute-start.3
  124.2 1.0 fusion.4
  125.2 3.1 copy.8
  128.4 0.6 collective-permute-done.3
  129.2 0.4 fusion.26
  129.7 0.3 fusion.20
  130.0 0.3 fusion.22
  130.3 0.3 convolution_add_fusion.6
  130.6 0.3 convolution_add_fusion.5
  131.5 0.3 convolution_add_fusion.2
  132.1 1.1 fusion.3
  133.2 475.1 %all-reduce.4.cloned.1.call-done = f32[3,3,256,256]{2,3,1,0:T(8,128)} async-done(((f32[3,3,256,256]{2,3,1,0:T(8,128)}), f32[3,3,256,256]{2,3,1,0:T(8,128)}) %all-reduce.4.cloned.1.call-update) | async-done | bytes 2359312 | tf_op jit(solution)/shard_map/psum | solution.py:85
  608.3 1.6 dynamic-slice_multiply_fusion
  (31 shorter events, 1.4 us)
Async XLA Ops:
  7.2 12.6 %copy-start = (bf16[1,8,128,256]{3,2,1,0:T(8,128)(2,1)S(1)}, bf16[1,8,128,256]{3,2,1,0:T(8,128)(2,1)}, u32[]{:S(2)}) copy-start(bf16[1,8,128,256]{3,2,1,0:T(8,128)(2,1)} %param.4) | copy-start | bytes 1572868
  7.2 94.1 %all-gather.2.cloned.1.call-start = ((), (), s32[]{:S(2)}) async-start(), calls=%async_computation | async-start | bytes 1253376 | tf_op jit(solution)/shard_map/all_gather | solution.py:50
  7.9 600.3 %all-reduce.4.cloned.1.call-start = ((), (), s32[]{:S(2)}) async-start(), calls=%async_computation.1 | async-start | bytes 4718592 | tf_op jit(solution)/shard_map/psum | solution.py:85
  8.8 5.4 collective-permute-start
  12.3 6.2 collective-permute-start.1
  22.1 84.1 %copy-start.2 = (bf16[1,8,128,256]{3,2,1,0:T(8,128)(2,1)}, bf16[1,8,128,256]{3,2,1,0:T(8,128)(2,1)S(1)}, u32[]{:S(2)}) copy-start(bf16[1,8,128,256]{3,2,1,0:T(8,128)(2,1)S(1)} %get-tuple-element.13) | copy-start | bytes 1572868
  101.3 1.4 copy-start.1
  101.3 1.7 copy-start.8
  103.0 1.0 copy-start.6
  103.4 1.1 copy-start.5
  104.8 1.0 copy-start.4
  106.2 1.0 copy-start.7
  107.2 0.8 copy-start.10
  107.6 1.0 copy-start.9
  115.7 2.1 copy-start.3
  119.8 8.6 %collective-permute-start.2 = (bf16[1,1,128,256]{3,2,1,0:T(8,128)(2,1)S(1)}, bf16[1,1,128,256]{3,2,1,0:T(8,128)(2,1)S(1)}, u32[]{:S(2)}, u32[]{:S(2)}) collective-permute-start(bf16[1,1,128,256]{3,2,1,0:T(8,128)(2,1)S(1)} %get-tuple-element.21), channel_id=1, source_target_pairs={{0,1},{1,2},{2,3},{3,4},{4,5},{5,6},{6,7},{7,8},{8,9},{9,10},{10,1... | collective-permute-start | bytes 196616 | tf_op jit(solution)/shard_map/ppermute | solution.py:19
  122.9 6.2 collective-permute-start.3
Sparse Core Ops, SparseCore 0:
  10.1 91.1 all-gather.1
  128.5 479.7 all-reduce.3
where the time goes:
time: 617 us
  waiting for transfers between devices  560 us (91%)
  matrix products  17 us (3%)
  between operations  14.3 us (2%)
  starting transfers between devices  9.17 us (1%)
  local copies, waits for them, and re-layouts  8.58 us (1%)
  other arithmetic  7.21 us (1%)
    psum x1, waiting for transfers between devices, on_device(): totals = lax.psum(partial_value, ('row', 'col'))  475 us
    all_gather x1, waiting for transfers between devices, on_device(): whole_kernel = lax.all_gather(weight, 'col', axis=3, tiled=True)  79.2 us
  transfers between devices with their start and end apart: 6, of which 5 were waited for; matrix products, arithmetic and copies ran while one was open for 2% of the time, Pallas kernels for 0%

commit v1 on v0

--- a/solution.py
+++ b/solution.py
@@ -82,7 +82,7 @@
                 )
             )
     partial_value = jnp.stack(pieces).reshape(3, 3, in_chan, out_chan)
-    totals = lax.psum(partial_value, ("row", "col"))
+    totals = lax.psum(lax.psum(partial_value, "col"), "row")
     col_share = out_chan // lax.axis_size("col")
     own_share = lax.dynamic_slice_in_dim(totals, lax.axis_index("col") * col_share, col_share, 3)
     pixels = img_count * lax.axis_size("row") * tile_rows * lax.axis_size("col") * tile_cols

time: 617 us -> 669 us (1.084)
  the two profiles are of different devices: /device:TPU:2 before, /device:TPU:1 now
where the time goes in v1:
time: 669 us; the launch traced here: 668 us
  waiting for transfers between devices  609 us (91%)
  matrix products  16.9 us (3%)
  between operations  14.1 us (2%)
  local copies, waits for them, and re-layouts  11.2 us (2%)
  starting transfers between devices  9.45 us (1%)
  other arithmetic  7.23 us (1%)
    psum x2, waiting for transfers between devices, on_device(): totals = lax.psum(lax.psum(partial_value, 'col'), 'row')  531 us
    all_gather x1, waiting for transfers between devices, on_device(): whole_kernel = lax.all_gather(weight, 'col', axis=3, tiled=True)  70.6 us
  transfers between devices with their start and end apart: 7, of which 5 were waited for; matrix products, arithmetic and copies ran while one was open for 1% of the time, Pallas kernels for 0%

profile of v1, /device:TPU:1, one launch (start us, length us, event | category | flops | bytes accessed | tf_op | source)
XLA Modules:
  0.0 668.3 jit_solution(7160664566902318417)
XLA Ops:
  7.2 0.7 all-gather.2.cloned.1.call-update
  8.0 0.9 fusion.29
  8.8 4.0 collective-permute-start
  12.9 1.3 collective-permute-start.1
  14.2 3.7 collective-permute-done.1
  17.9 1.2 select_maximum_fusion.2
  19.1 1.0 pad_maximum_fusion.2
  20.2 1.4 fusion.27
  21.5 70.6 %all-gather.2.cloned.1.call-done = bf16[3,3,256,256]{2,3,1,0:T(8,128)(2,1)} async-done(((bf16[3,3,256,16]{2,3,1,0:T(8,128)(2,1)}), bf16[3,3,256,256]{2,3,1,0:T(8,128)(2,1)}) %all-gather.2.cloned.1.call-update) | async-done | bytes 1179664 | tf_op jit(solution)/shard_map/all_gather | solution.py:50
  92.2 1.4 fusion.21
  93.5 0.3 fusion.23
  93.9 0.3 convolution_add_fusion.13
  94.3 0.7 copy-done.6
  94.9 0.3 convolution_add_fusion.12
  95.3 0.3 convolution_add_fusion.11
  95.7 0.3 convolution_add_fusion.10
  96.0 0.7 copy-done.4
  96.7 0.3 convolution_add_fusion.9
  97.1 0.3 convolution_add_fusion.8
  97.4 0.7 copy-done.11
  98.1 0.4 fusion.30
  98.5 0.4 multiply_reduce_fusion.1
  98.9 0.6 copy-done.13
  99.6 1.9 fusion.24
  101.5 0.8 multiply_convert_fusion
  102.3 1.0 fusion.12
  103.4 1.0 fusion.11
  104.4 1.0 fusion.10
  105.4 1.0 fusion.9
  106.5 1.1 fusion.8
  107.5 1.0 fusion.7
  108.6 1.0 fusion.6
  109.6 1.1 fusion.5
  110.7 1.0 fusion.4
  111.7 3.0 copy.8
  114.8 2.7 collective-permute-start.2
  117.6 1.3 collective-permute-start.3
  118.9 3.7 collective-permute-done.3
  122.8 1.6 fusion.26
  124.6 167.9 %all-reduce.5.cloned.1.call-done = f32[3,3,256,256]{2,3,1,0:T(8,128)} async-done(((f32[3,3,256,256]{2,3,1,0:T(8,128)}), f32[3,3,256,256]{2,3,1,0:T(8,128)}) %all-reduce.5.cloned.1.call-update) | async-done | bytes 2359312 | tf_op jit(solution)/shard_map/psum | solution.py:85
  292.9 0.3 convolution_add_fusion.6
  293.2 0.7 copy-done.10
  293.9 0.3 convolution_add_fusion.5
  294.9 0.7 copy-done.8
  295.6 0.3 convolution_add_fusion.2
  296.3 1.1 fusion.3
  297.4 362.8 %all-reduce.7.cloned.1.call-done = f32[3,3,256,256]{2,3,1,0:T(8,128)} async-done(((f32[3,3,256,256]{2,3,1,0:T(8,128)}), f32[3,3,256,256]{2,3,1,0:T(8,128)}) %all-reduce.7.cloned.1.call-update) | async-done | bytes 2359312 | tf_op jit(solution)/shard_map/psum | solution.py:85
  660.2 1.6 dynamic-slice_multiply_fusion
  (42 shorter events, 2.1 us)
Async XLA Ops:
  7.2 12.0 %copy-start = (bf16[1,8,128,256]{3,2,1,0:T(8,128)(2,1)S(1)}, bf16[1,8,128,256]{3,2,1,0:T(8,128)(2,1)}, u32[]{:S(2)}) copy-start(bf16[1,8,128,256]{3,2,1,0:T(8,128)(2,1)} %param.4) | copy-start | bytes 1572868
  7.2 85.0 %all-gather.2.cloned.1.call-start = ((), (), s32[]{:S(2)}) async-start(), calls=%async_computation | async-start | bytes 1253376 | tf_op jit(solution)/shard_map/all_gather | solution.py:50
  7.9 284.6 %all-reduce.5.cloned.1.call-start = ((), (), s32[]{:S(2)}) async-start(), calls=%async_computation.1 | async-start | bytes 4718592 | tf_op jit(solution)/shard_map/psum | solution.py:85
  8.8 5.4 collective-permute-start
  12.9 5.0 collective-permute-start.1
  21.5 75.5 %copy-start.2 = (bf16[1,8,128,256]{3,2,1,0:T(8,128)(2,1)}, bf16[1,8,128,256]{3,2,1,0:T(8,128)(2,1)S(1)}, u32[]{:S(2)}) copy-start(bf16[1,8,128,256]{3,2,1,0:T(8,128)(2,1)S(1)} %get-tuple-element.13) | copy-start | bytes 1572868
  92.2 1.4 copy-start.1
  92.2 1.7 copy-start.12
  93.9 1.0 copy-start.6
  94.2 1.1 copy-start.5
  95.7 1.0 copy-start.4
  97.0 1.0 copy-start.11
  98.1 0.8 copy-start.14
  98.5 1.0 copy-start.13
  106.5 2.1 copy-start.3
  114.8 545.4 %all-reduce.7.cloned.1.call-start = ((), (), s32[]{:S(2)}) async-start(), calls=%async_computation.2 | async-start | bytes 4718592 | tf_op jit(solution)/shard_map/psum | solution.py:85
  114.8 4.0 collective-permute-start.2
  117.6 5.0 collective-permute-start.3
  292.9 1.0 copy-start.10
  293.2 1.1 copy-start.9
  294.6 1.0 copy-start.8
  294.9 1.1 copy-start.7
Sparse Core Ops, SparseCore 0:
  10.1 82.0 all-gather.1
  114.9 177.5 all-reduce.4
  295.4 364.6 all-reduce.6
